TPU v7x, 512 devices: a whole 4x8x8 slice. The times are simulated.
512 devices in a mesh: ep: 128 (over y, z, core), dp: 4 (over x).
Axes of the slice: x: 4, y: 8, z: 8, core: 2. Of those that a mesh axis runs over, the one named last changes fastest.
Arguments:
- tokens: bfloat16 [2, 2048, 3584], P(None, ('ep', 'dp')), may hold values from -6 to 6
- routing: int32 [2, 2048, 8], P(None, 'ep'), may hold values from 0 to 127, all different within a row; in each aligned block of 16 rows (0 to 15, 16 to 31, ..., all dimensions but the last counted through in order) at most 2 rows name the same one
- gate_values: float32 [2, 2048, 8], P(None, 'ep'), may hold values from 0.05 to 0.5
- held_weight: bfloat16 [128, 3584, 1024], P('ep', None, 'dp'), may hold values from -0.09375 to 0.09375
- scale_table: float32 [128, 28, 8], P(None, None, 'dp'), may hold values from 0.25 to 4
- old_expert: int32 [128], replicated, may hold values from 0 to 127, as said below
- new_expert: int32 [128], replicated, may hold values from 0 to 127, as said below
Outputs:
- combined: bfloat16 [2, 2048, 1024], P(None, 'ep', 'dp')
- moved_weight: bfloat16 [128, 3584, 1024], P('ep', None, 'dp')
Inputs may be any that keep to these rules, and one draw needn't show every extreme that they name: `routing`: each row names 8 different experts; in each aligned block of 16 token rows of a step no expert is named by more than 2 rows. `old_expert`: A permutation of the experts over the slots. `new_expert`: A permutation of the experts over the slots; it equals old_expert except at exactly 32 slots, whose experts are permuted among themselves so that each of them changes.
All inputs are finite; a program needn't handle non-finite values.
Results may differ from a plain program's by a relative error of at most 0.0039.
Values may be sent and summed in bfloat16 or wider, within the bound.
No kernel may reach another device: no remote copies, remote signals or barrier semaphores. Data moves between devices by JAX's collectives and lax.ppermute only.
A program may use at most 64 MiB of HBM per device.

v0:
```python
import jax
import jax.numpy as jnp
from jax import lax
from jax.sharding import PartitionSpec as P


def inverse_place(expert_at):
    count = expert_at.shape[0]
    labels = jnp.arange(count, dtype=jnp.int32)
    match = expert_at[None, :] == labels[:, None]
    return jnp.sum(jnp.where(match, labels[None, :], 0), axis=1)


def source_slots(old_expert, new_expert):
    labels = jnp.arange(old_expert.shape[0], dtype=jnp.int32)
    match = old_expert[None, :] == new_expert[:, None]
    return jnp.sum(jnp.where(match, labels[None, :], 0), axis=1)


def route_targets(routing, owners, peers, capacity):
    steps, group_size, top_count = routing.shape
    labels = jnp.arange(peers, dtype=jnp.int32)
    pair_ids = routing.reshape(steps, group_size * top_count)
    onehot = (pair_ids[:, :, None] == labels[None, None, :]).astype(jnp.int32)
    before = jnp.cumsum(onehot, axis=1) - onehot
    rank = jnp.sum(before * onehot, axis=2)
    slot = owners[pair_ids]
    step = jnp.arange(steps, dtype=jnp.int32)[:, None]
    return (slot * steps + step) * capacity + rank


def shards(tokens, routing, gate_values, held_weight, scale_table, old_expert, new_expert):
    peers = lax.axis_size("ep")
    n_dp = lax.axis_size("dp")
    my_slot = lax.axis_index("ep")
    my_dp = lax.axis_index("dp")
    steps, group_size, top_count = routing.shape
    capacity = 2
    old_block = held_weight[0]
    rows, cols = old_block.shape
    row_part = rows // n_dp
    blk = rows // scale_table.shape[1]
    owners = inverse_place(old_expert)
    sources = source_slots(old_expert, new_expert)
    w_rows = lax.all_to_all(old_block, "dp", split_axis=0, concat_axis=1, tiled=True)
    my_scales = lax.all_gather(scale_table[old_expert[my_slot]], "dp", axis=1, tiled=True)
    row_blocks = row_part // blk
    my_scales = lax.dynamic_slice_in_dim(my_scales, my_dp * row_blocks, row_blocks, axis=0)
    widened = jnp.repeat(jnp.repeat(my_scales, blk, axis=0), blk, axis=1)
    w32 = w_rows.astype(jnp.float32) * widened
    w_hi = w32.astype(jnp.bfloat16)
    w_lo = (w32 - w_hi.astype(jnp.float32)).astype(jnp.bfloat16)
    feats = lax.all_to_all(tokens, "dp", split_axis=2, concat_axis=1, tiled=True)
    target = route_targets(routing, owners, peers, capacity)
    token_of = jnp.broadcast_to(
        jnp.arange(group_size, dtype=jnp.int32)[None, :, None], (steps, group_size, top_count)
    ).reshape(steps, -1)
    step_of = jnp.broadcast_to(jnp.arange(steps, dtype=jnp.int32)[:, None], token_of.shape)
    pick = (
        jnp.zeros((peers * steps * capacity,), jnp.int32)
        .at[target.reshape(-1)]
        .set((step_of * group_size + token_of).reshape(-1))
    )
    send_tokens = feats.reshape(steps * group_size, row_part)[pick]
    send_tokens = send_tokens.reshape(peers, steps * capacity * row_part)
    pieces = old_block.reshape(peers, rows // peers * cols)
    first = lax.all_to_all(
        jnp.concatenate([pieces, send_tokens], axis=1),
        "ep",
        split_axis=0,
        concat_axis=0,
        tiled=True,
    )
    piece_len = pieces.shape[1]
    gathered_pieces = jnp.take(first[:, :piece_len], sources, axis=0)
    arrived = first[:, piece_len:].reshape(peers * steps * capacity, row_part)
    partial = jnp.dot(arrived, w_hi, preferred_element_type=jnp.float32) + jnp.dot(
        arrived, w_lo, preferred_element_type=jnp.float32
    )
    hidden = lax.psum_scatter(partial, "dp", scatter_dimension=1, tiled=True)
    act = jax.nn.silu(hidden).astype(jnp.bfloat16)
    act = act.reshape(peers, steps * capacity * act.shape[1])
    second = lax.all_to_all(
        jnp.concatenate([gathered_pieces, act], axis=1),
        "ep",
        split_axis=0,
        concat_axis=0,
        tiled=True,
    )
    new_block = second[:, :piece_len].reshape(rows, cols)
    returned = second[:, piece_len:].reshape(peers * steps * capacity, -1)
    picked = returned[target].astype(jnp.float32).reshape(steps, group_size, top_count, -1)
    combined = jnp.sum(gate_values[:, :, :, None] * picked, axis=2).astype(jnp.bfloat16)
    return (combined, new_block[None])


def solution(mesh):
    placed = (
        P(None, ("ep", "dp"), None),
        P(None, "ep", None),
        P(None, "ep", None),
        P("ep", None, "dp"),
        P(None, None, "dp"),
        P(),
        P(),
    )
    return jax.shard_map(
        shards,
        mesh=mesh,
        in_specs=placed,
        out_specs=(P(None, "ep", "dp"), P("ep", None, "dp")),
        check_vma=False,
    )
```

profile of v0, /device:TPU:1, one launch (start us, length us, event | category | flops | bytes accessed | tf_op | source)
XLA Modules:
  0.0 288.5 jit_solution(11411212066454031922)
XLA Ops:
  7.2 3.8 %copy.43 = bf16[2,4,3584]{1,0,2:T(2,128)(2,1)S(1)} copy(bf16[2,4,3584]{2,1,0:T(4,128)(2,1)} %param.7) | data formatting | bytes 114688 | tf_op args[0]
  11.0 4.3 %reshape.277 = bf16[4,2,3584]{2,1,0:T(2,128)(2,1)} reshape(bf16[3584,2,4]{2,1,0:T(2,128)(2,1)S(1)} %bitcast.65) | data formatting | bytes 114688
  15.3 4.8 %all-to-all-start = ((bf16[4,2,3584]{2,1,0:T(2,128)(2,1)}), bf16[4,2,3584]{2,1,0:T(2,128)(2,1)S(1)}, u32[]{:S(2)}, u32[]{:S(2)}) async-start(bf16[4,2,3584]{2,1,0:T(2,128)(2,1)} %reshape.277), calls=%async_computation | async-start | bytes 114688 | tf_op jit(solution)/shard_map/all_to_all | solution.py:53
  20.1 0.1 copy.45
  20.2 0.1 eq.44
  20.3 0.1 reshape.216
  20.4 0.1 fusion.1
  20.5 0.2 reduce_window_sum.11
  20.7 0.2 select_reduce_fusion
  20.9 0.2 select_reduce_fusion.2
  21.1 1.9 gather_fusion
  23.0 0.1 reshape.217
  23.1 0.1 bitcast_add_fusion.2
  23.1 1.4 scatter_custom_fusion
  24.6 4.5 %reshape_squeeze.3 = bf16[128,7168]{1,0:T(8,128)(2,1)} reshape(bf16[1,3584,256]{2,1,0:T(8,128)(2,1)} %param.10) | data formatting | bytes 3670016 | tf_op jit(solution)/shard_map/reshape;squeeze | solution.py:66
  29.0 4.6 %all-to-all-start.2 = ((bf16[4,896,256]{2,1,0:T(8,128)(2,1)}), bf16[4,896,256]{2,1,0:T(8,128)(2,1)}, u32[]{:S(2)}, u32[]{:S(2)}) async-start(bf16[4,896,256]{2,1,0:T(8,128)(2,1)} %bitcast.10), calls=%async_computation.2 | async-start | bytes 3670016 | tf_op jit(solution)/shard_map/all_to_all | solution.py:45
  33.6 3.9 %reshape.278 = bf16[3584,2,4]{2,1,0:T(2,128)(2,1)S(1)} reshape(bf16[4,2,3584]{2,1,0:T(2,128)(2,1)S(1)} %all-to-all-done) | data formatting | bytes 114688
  37.6 1.3 copy.44
  38.9 2.1 gather_fusion.1
  41.0 1.5 reshape.218
  42.5 2.0 maximum_bitcast_fusion
  44.4 0.5 broadcast.167
  44.9 3.4 %reduce = bf16[128,10752]{1,0:T(8,128)(2,1)} reduce(bf16[128,1,10752]{2,0,1:T(8,128)(2,1)S(1)} %maximum_bitcast_fusion, bf16[]{:T(256)} %broadcast.167), dimensions={1}, to_apply=%copy.47.reduce_sub_computation | reduce | bytes 5505026 | tf_op jit(solution)/shard_map/all_to_all | solution.py:67
  48.4 4.2 %reshape.279 = bf16[128,2,5376]{2,1,0:T(2,128)(2,1)} reshape(bf16[128,10752]{1,0:T(8,128)(2,1)} %reduce) | data formatting | bytes 5505024
  52.6 22.5 %all-to-all-start.1 = ((bf16[128,2,5376]{2,1,0:T(2,128)(2,1)}), bf16[128,2,5376]{2,1,0:T(2,128)(2,1)S(1)}, u32[]{:S(2)}, u32[]{:S(2)}) async-start(bf16[128,2,5376]{2,1,0:T(2,128)(2,1)} %reshape.279), calls=%async_computation.1 | async-start | bytes 5505024 | tf_op jit(solution)/shard_map/all_to_all | solution.py:67
  75.1 0.0 reduce-scatter.2.cloned.1.call-start
  75.1 0.6 dynamic_slice.9
  77.7 0.1 constant_dynamic-slice_fusion
  77.8 0.1 copy.54
  77.9 6.9 %all-gather = f32[1,28,8]{1,0,2:T(1,128)S(1)} all-gather(f32[1,28,2]{1,0,2:T(1,128)S(1)} %copy.54), channel_id=2, replica_groups=mesh['ep'=128,'dp'=4] {'dp'}, dimensions={2}, use_global_device_ids=true | all-gather | bytes 1120 | tf_op jit(solution)/shard_map/all_gather | solution.py:46
  84.8 0.1 constant_dynamic-slice_fusion.1
  84.9 0.1 copy.55
  85.0 0.1 broadcast_bitcast_fusion
  85.0 3.6 %convert_bitcast_fusion = f32[896,4,256]{2,0,1:T(8,128)} fusion(bf16[4,896,256]{2,1,0:T(8,128)(2,1)} %all-to-all-done.2), kind=kLoop, calls=%fused_computation.5 | loop fusion | flops 917504 | bytes 5505024 | tf_op jit(solution)/shard_map/convert_element_type | solution.py:50
  88.7 4.6 %copy.48 = f32[896,4,256]{0,2,1:T(8,128)} copy(f32[896,4,256]{2,0,1:T(8,128)} %convert_bitcast_fusion) | data formatting | bytes 7340032 | tf_op jit(solution)/shard_map/convert_element_type | solution.py:50
  93.3 4.5 %subtract_convert_fusion = (bf16[896,8,128]{0,2,1:T(8,128)(2,1)}, bf16[896,8,128]{0,2,1:T(8,128)(2,1)}) fusion(f32[896,8,128]{0,2,1:T(8,128)} %bitcast.59, f32[896,8]{0,1:T(8,128)S(1)} %broadcast_bitcast_fusion), kind=kLoop, calls=%fused_computation.6 | loop fusion | flops 4587520 | bytes 7368704 | tf_op jit(solution)/shard_map/convert_element_type | solution.py:52
  97.8 42.8 %all-to-all-done.1 = bf16[128,2,5376]{2,1,0:T(2,128)(2,1)S(1)} async-done(((bf16[128,2,5376]{2,1,0:T(2,128)(2,1)}), bf16[128,2,5376]{2,1,0:T(2,128)(2,1)S(1)}, u32[]{:S(2)}, u32[]{:S(2)}) %all-to-all-start.1) | async-done | bytes 2752544 | tf_op jit(solution)/shard_map/all_to_all | solution.py:67
  140.6 7.1 %reshape.280 = bf16[128,1,10752]{2,1,0:T(2,128)(2,1)} reshape(bf16[128,2,5376]{2,1,0:T(2,128)(2,1)S(1)} %all-to-all-done.1) | data formatting | bytes 5505024
  147.7 2.9 %copy.58 = bf16[128,1,10752]{2,0,1:T(8,128)(2,1)S(1)} copy(bf16[128,1,10752]{2,1,0:T(2,128)(2,1)} %reshape.280) | data formatting | bytes 5505024
  150.7 1.5 copy-done.2
  152.2 0.1 slice.25
  152.3 1.5 reshape.219
  153.8 2.6 fusion.10
  156.4 2.6 convolution_add_fusion
  159.0 0.0 reduce-scatter.2.cloned.1.call-update
  159.1 1.6 slice.24
  160.7 2.9 %gather_fusion.2 = bf16[128,7168]{1,0:T(8,128)(2,1)} fusion(bf16[128,7168]{1,0:T(8,128)(2,1)S(1)} %slice.24, s32[1024]{0:T(1024)S(1)} %pad_clamp_fusion.1), kind=kCustom, calls=%fused_computation.2 | custom fusion | bytes 3670528 | tf_op jit(solution)/shard_map/jit(_take)/gather | solution.py:75
  163.6 3.0 %broadcast_select_fusion = bf16[128,7168]{1,0:T(8,128)(2,1)} fusion(bf16[128,7168]{1,0:T(8,128)(2,1)} %gather_fusion.2, pred[128]{0:T(512)(128)(4,1)S(1)} %compare_and_fusion), kind=kLoop, calls=%fused_computation.12 | loop fusion | flops 917504 | bytes 3670144 | tf_op jit(solution)/shard_map/jit(_take)/select_n | solution.py:75
  166.6 21.2 %reduce-scatter.2.cloned.1.call-done = f32[512,256]{1,0:T(8,128)} async-done(((f32[512,1024]{1,0:T(8,128)}), f32[512,256]{1,0:T(8,128)}) %reduce-scatter.2.cloned.1.call-update) | async-done | bytes 524304 | tf_op jit(solution)/shard_map/reduce_scatter | solution.py:80
  187.7 1.2 multiply_convert_fusion.1
  188.9 0.2 reshape.221
  189.1 1.6 maximum_bitcast_fusion.1
  190.7 2.9 %reduce.1 = bf16[128,8192]{1,0:T(8,128)(2,1)} reduce(bf16[128,1,8192]{2,0,1:T(8,128)(2,1)S(1)} %maximum_bitcast_fusion.1, bf16[]{:T(256)} %broadcast.167), dimensions={1}, to_apply=%copy.51.reduce_sub_computation | reduce | bytes 4194306 | tf_op jit(solution)/shard_map/all_to_all | solution.py:83
  193.7 4.5 %reshape.281 = bf16[128,2,4096]{2,1,0:T(2,128)(2,1)} reshape(bf16[128,8192]{1,0:T(8,128)(2,1)} %reduce.1) | data formatting | bytes 4194304
  198.2 14.5 %all-to-all-start.3 = ((bf16[128,2,4096]{2,1,0:T(2,128)(2,1)}), bf16[128,2,4096]{2,1,0:T(2,128)(2,1)S(1)}, u32[]{:S(2)}, u32[]{:S(2)}) async-start(bf16[128,2,4096]{2,1,0:T(2,128)(2,1)} %reshape.281), calls=%async_computation.4 | async-start | bytes 4194304 | tf_op jit(solution)/shard_map/all_to_all | solution.py:83
  212.7 0.1 copy.42
  212.8 52.0 %all-to-all-done.3 = bf16[128,2,4096]{2,1,0:T(2,128)(2,1)S(1)} async-done(((bf16[128,2,4096]{2,1,0:T(2,128)(2,1)}), bf16[128,2,4096]{2,1,0:T(2,128)(2,1)S(1)}, u32[]{:S(2)}, u32[]{:S(2)}) %all-to-all-start.3) | async-done | bytes 2097184 | tf_op jit(solution)/shard_map/all_to_all | solution.py:83
  264.8 6.8 %reshape.282 = bf16[128,1,8192]{2,1,0:T(2,128)(2,1)} reshape(bf16[128,2,4096]{2,1,0:T(2,128)(2,1)S(1)} %all-to-all-done.3) | data formatting | bytes 4194304
  271.6 4.5 %copy.59 = bf16[128,1,8192]{2,0,1:T(8,128)(2,1)S(1)} copy(bf16[128,1,8192]{2,1,0:T(2,128)(2,1)} %reshape.282) | data formatting | bytes 4194304
  276.1 0.1 slice.27
  276.2 0.2 reshape.222
  276.4 3.3 %broadcast_in_dim_reshape.4 = bf16[1,3584,256]{2,1,0:T(8,128)(2,1)} reshape(bf16[128,7168]{1,0:T(8,128)(2,1)S(1)} %slice.27) | data formatting | bytes 3670016 | tf_op jit(solution)/shard_map/broadcast_in_dim;reshape | solution.py:94
  279.7 1.1 gather_fusion.3
  280.8 0.8 fusion
  (36 shorter events, 0.2 us)
Async XLA Ops:
  7.2 70.5 %copy-start = (f32[128,28,2]{0,2,1:T(2,128)S(1)}, f32[128,28,2]{0,2,1:T(2,128)}, u32[]{:S(2)}) copy-start(f32[128,28,2]{0,2,1:T(2,128)} %param.11) | copy-start | bytes 86020
  7.2 12.9 %copy-start.6 = (s32[2,16,8]{1,2,0:T(8,128)S(1)}, s32[2,16,8]{1,2,0:T(8,128)}, u32[]{:S(2)}) copy-start(s32[2,16,8]{1,2,0:T(8,128)} %param.8) | copy-start | bytes 3076
  7.2 13.7 %copy-start.9 = (s32[128]{0:T(128)S(1)}, s32[128]{0:T(128)}, u32[]{:S(2)}) copy-start(s32[128]{0:T(128)} %param.12) | copy-start | bytes 1540
  7.2 13.7 %copy-start.8 = (s32[128]{0:T(128)S(1)}, s32[128]{0:T(128)}, u32[]{:S(2)}) copy-start(s32[128]{0:T(128)} %param.13) | copy-start | bytes 1540
  15.3 13.8 %all-to-all-start = ((bf16[4,2,3584]{2,1,0:T(2,128)(2,1)}), bf16[4,2,3584]{2,1,0:T(2,128)(2,1)S(1)}, u32[]{:S(2)}, u32[]{:S(2)}) async-start(bf16[4,2,3584]{2,1,0:T(2,128)(2,1)} %reshape.277), calls=%async_computation | async-start | bytes 114688 | tf_op jit(solution)/shard_map/all_to_all | solution.py:53
  29.0 23.6 %all-to-all-start.2 = ((bf16[4,896,256]{2,1,0:T(8,128)(2,1)}), bf16[4,896,256]{2,1,0:T(8,128)(2,1)}, u32[]{:S(2)}, u32[]{:S(2)}) async-start(bf16[4,896,256]{2,1,0:T(8,128)(2,1)} %bitcast.10), calls=%async_computation.2 | async-start | bytes 3670016 | tf_op jit(solution)/shard_map/all_to_all | solution.py:45
  52.6 88.0 %all-to-all-start.1 = ((bf16[128,2,5376]{2,1,0:T(2,128)(2,1)}), bf16[128,2,5376]{2,1,0:T(2,128)(2,1)S(1)}, u32[]{:S(2)}, u32[]{:S(2)}) async-start(bf16[128,2,5376]{2,1,0:T(2,128)(2,1)} %reshape.279), calls=%async_computation.1 | async-start | bytes 5505024 | tf_op jit(solution)/shard_map/all_to_all | solution.py:67
  75.1 112.7 %reduce-scatter.2.cloned.1.call-start = ((), (), s32[]{:S(2)}) async-start(), calls=%async_computation.5 | async-start | bytes 2621440 | tf_op jit(solution)/shard_map/reduce_scatter | solution.py:80
  150.6 1.6 copy-start.2
  150.6 3.1 %copy-start.4 = (bf16[896,8,128]{0,2,1:T(8,128)(2,1)S(1)}, bf16[896,8,128]{0,2,1:T(8,128)(2,1)}, u32[]{:S(2)}) copy-start(bf16[896,8,128]{0,2,1:T(8,128)(2,1)} %get-tuple-element.5) | copy-start | bytes 5505028
  153.8 2.6 copy-start.3
  153.8 2.6 copy-start.5
  198.2 14.5 %copy-start.7 = (f32[2,16,8]{1,2,0:T(8,128)S(1)}, f32[2,16,8]{1,2,0:T(8,128)}, u32[]{:S(2)}) copy-start(f32[2,16,8]{1,2,0:T(8,128)} %param.9) | copy-start | bytes 3076
  198.2 66.6 %all-to-all-start.3 = ((bf16[128,2,4096]{2,1,0:T(2,128)(2,1)}), bf16[128,2,4096]{2,1,0:T(2,128)(2,1)S(1)}, u32[]{:S(2)}, u32[]{:S(2)}) async-start(bf16[128,2,4096]{2,1,0:T(2,128)(2,1)} %reshape.281), calls=%async_computation.4 | async-start | bytes 4194304 | tf_op jit(solution)/shard_map/all_to_all | solution.py:83
  276.2 5.4 %copy-start.1 = (f32[128,28,2]{0,2,1:T(2,128)S(1)}, f32[128,28,2]{0,2,1:T(2,128)}, u32[]{:S(2)}) copy-start(f32[128,28,2]{0,2,1:T(2,128)} %param.11) | copy-start | bytes 86020
Sparse Core Ops, SparseCore 0:
  159.1 28.5 reduce-scatter.1
where the time goes:
time: 290 us; the launch traced here: 288 us
  waiting for transfers between devices  116 us (40%)
  local copies, waits for them, and re-layouts  73.7 us (25%)
  starting transfers between devices  46.4 us (16%)
  other arithmetic  23.8 us (8%)
  between operations  16.3 us (6%)
  blocking collectives  6.95 us (2%)
  matrix products  5.21 us (2%)
    all_to_all x1, waiting for transfers between devices, shards(): lax.all_to_all(jnp.concatenate([gathered_pieces, act], axis=1), 'ep', spl...  52 us
    unnamed x33, local copies, waits for them, and re-layouts  43.8 us
    all_to_all x1, waiting for transfers between devices, shards(): lax.all_to_all(jnp.concatenate([pieces, send_tokens], axis=1), 'ep', spli...  42.8 us
    all_to_all x1, starting transfers between devices, shards(): lax.all_to_all(jnp.concatenate([pieces, send_tokens], axis=1), 'ep', spli...  22.5 us
    reduce_scatter x1, waiting for transfers between devices, shards(): hidden = lax.psum_scatter(partial, 'dp', scatter_dimension=1, tiled=True)  21.2 us
    all_to_all x1, starting transfers between devices, shards(): lax.all_to_all(jnp.concatenate([gathered_pieces, act], axis=1), 'ep', spl...  14.5 us
    all_gather x1, blocking collectives, shards(): lax.all_gather(scale_table[old_expert[my_slot]], 'dp', axis=1, tiled=True)  6.95 us
  transfers between devices with their start and end apart: 5, of which 3 were waited for; matrix products, arithmetic and copies ran while one was open for 17% of the time, Pallas kernels for 0%

commit v1 on v0

--- a/solution.py
+++ b/solution.py
@@ -43,7 +43,10 @@
     owners = inverse_place(old_expert)
     sources = source_slots(old_expert, new_expert)
     w_rows = lax.all_to_all(old_block, "dp", split_axis=0, concat_axis=1, tiled=True)
-    my_scales = lax.all_gather(scale_table[old_expert[my_slot]], "dp", axis=1, tiled=True)
+    frame = scale_table[old_expert[my_slot]]
+    my_scales = jnp.concatenate(
+        jax.lax.all_to_all(jnp.stack([frame] * jax.lax.axis_size("dp")), "dp", 0, 0), 1
+    )
     row_blocks = row_part // blk
     my_scales = lax.dynamic_slice_in_dim(my_scales, my_dp * row_blocks, row_blocks, axis=0)
     widened = jnp.repeat(jnp.repeat(my_scales, blk, axis=0), blk, axis=1)

time: 290 us -> 299 us (1.031)
  waiting for transfers between devices: 116 us -> 125 us
  blocking collectives: 6.95 us -> 0 us
  starting transfers between devices: 46.4 us -> 50.9 us
    all_to_all x1, waiting for transfers between devices: 42.8 us -> 52.3 us  [shards(): lax.all_to_all(jnp.concatenate([pieces, send_tokens], axis=1), 'ep', spli...]
    all_gather x1 -> x0, blocking collectives: 6.95 us -> none  [shards(): lax.all_gather(scale_table[old_expert[my_slot]], 'dp', axis=1, tiled=True)]
    all_to_all x0 -> x1, starting transfers between devices: none -> 4.83 us  [shards(): jax.lax.all_to_all(jnp.stack([frame] * jax.lax.axis_size('dp')), 'dp', 0, 0)]
    unnamed x33 -> x25, local copies, waits for them, and re-layouts: 43.8 us -> 44.3 us
  transfers between devices with their start and end apart: 5 -> 6, of which waited for: 3 -> 3; matrix products, arithmetic and copies ran while one was open for 17% -> 19% of each run, Pallas kernels for 0% -> 0%
where the time goes in v1:
time: 299 us; the launch traced here: 298 us
  waiting for transfers between devices  125 us (42%)
  local copies, waits for them, and re-layouts  75.6 us (25%)
  starting transfers between devices  50.9 us (17%)
  other arithmetic  24.5 us (8%)
  between operations  16.3 us (5%)
  matrix products  5.22 us (2%)
    all_to_all x1, waiting for transfers between devices, shards(): lax.all_to_all(jnp.concatenate([pieces, send_tokens], axis=1), 'ep', spli...  52.3 us
    all_to_all x1, waiting for transfers between devices, shards(): lax.all_to_all(jnp.concatenate([gathered_pieces, act], axis=1), 'ep', spl...  52 us
    unnamed x25, local copies, waits for them, and re-layouts  44.3 us
    all_to_all x1, starting transfers between devices, shards(): lax.all_to_all(jnp.concatenate([pieces, send_tokens], axis=1), 'ep', spli...  22.5 us
    reduce_scatter x1, waiting for transfers between devices, shards(): hidden = lax.psum_scatter(partial, 'dp', scatter_dimension=1, tiled=True)  21.2 us
    all_to_all x1, starting transfers between devices, shards(): lax.all_to_all(jnp.concatenate([gathered_pieces, act], axis=1), 'ep', spl...  14.5 us
  transfers between devices with their start and end apart: 6, of which 3 were waited for; matrix products, arithmetic and copies ran while one was open for 19% of the time, Pallas kernels for 0%

profile of v1, /device:TPU:1, one launch (start us, length us, event | category | flops | bytes accessed | tf_op | source)
XLA Modules:
  0.0 298.0 jit_solution(16808319060570230638)
XLA Ops:
  7.2 1.2 dynamic_slice.11
  10.4 0.1 constant_dynamic-slice_fusion
  10.5 0.1 copy.52
  10.6 0.6 stack.3
  11.2 4.8 %all-to-all-start.3 = ((f32[4,28,2]{1,2,0:T(2,128)}), f32[4,28,2]{1,2,0:T(2,128)S(1)}, u32[]{:S(2)}, u32[]{:S(2)}) async-start(f32[4,28,2]{1,2,0:T(2,128)} %stack.3), calls=%async_computation.3 | async-start | bytes 8192 | tf_op jit(solution)/shard_map/all_to_all | solution.py:48
  16.0 0.8 copy.48
  16.8 0.1 eq.44
  16.9 0.1 reshape.223
  17.0 0.1 fusion.1
  17.1 0.2 reduce_window_sum.11
  17.3 0.2 select_reduce_fusion
  17.4 0.9 select_reduce_fusion.2
  18.3 0.1 reshape.224
  18.4 1.9 gather_fusion
  20.3 0.1 bitcast_add_fusion.2
  20.4 3.7 %copy.46 = bf16[2,4,3584]{1,0,2:T(2,128)(2,1)S(1)} copy(bf16[2,4,3584]{2,1,0:T(4,128)(2,1)} %param.7) | data formatting | bytes 114688 | tf_op args[0]
  24.2 4.3 %reshape.284 = bf16[4,2,3584]{2,1,0:T(2,128)(2,1)} reshape(bf16[3584,2,4]{2,1,0:T(2,128)(2,1)S(1)} %bitcast.68) | data formatting | bytes 114688
  28.4 1.4 scatter_custom_fusion
  29.8 4.2 %all-to-all-start = ((bf16[4,2,3584]{2,1,0:T(2,128)(2,1)}), bf16[4,2,3584]{2,1,0:T(2,128)(2,1)S(1)}, u32[]{:S(2)}, u32[]{:S(2)}) async-start(bf16[4,2,3584]{2,1,0:T(2,128)(2,1)} %reshape.284), calls=%async_computation | async-start | bytes 114688 | tf_op jit(solution)/shard_map/all_to_all | solution.py:56
  34.1 4.5 %reshape_squeeze.3 = bf16[128,7168]{1,0:T(8,128)(2,1)} reshape(bf16[1,3584,256]{2,1,0:T(8,128)(2,1)} %param.10) | data formatting | bytes 3670016 | tf_op jit(solution)/shard_map/reshape;squeeze | solution.py:69
  38.6 4.6 %all-to-all-start.2 = ((bf16[4,896,256]{2,1,0:T(8,128)(2,1)}), bf16[4,896,256]{2,1,0:T(8,128)(2,1)}, u32[]{:S(2)}, u32[]{:S(2)}) async-start(bf16[4,896,256]{2,1,0:T(8,128)(2,1)} %bitcast.10), calls=%async_computation.2 | async-start | bytes 3670016 | tf_op jit(solution)/shard_map/all_to_all | solution.py:45
  43.2 3.9 %reshape.285 = bf16[3584,2,4]{2,1,0:T(2,128)(2,1)S(1)} reshape(bf16[4,2,3584]{2,1,0:T(2,128)(2,1)S(1)} %all-to-all-done) | data formatting | bytes 114688
  47.1 1.3 copy.47
  48.4 2.1 gather_fusion.1
  50.5 1.5 reshape.225
  52.0 2.0 maximum_bitcast_fusion
  53.9 0.5 broadcast.168
  54.5 3.4 %reduce = bf16[128,10752]{1,0:T(8,128)(2,1)} reduce(bf16[128,1,10752]{2,0,1:T(8,128)(2,1)S(1)} %maximum_bitcast_fusion, bf16[]{:T(256)} %broadcast.168), dimensions={1}, to_apply=%copy.50.reduce_sub_computation | reduce | bytes 5505026 | tf_op jit(solution)/shard_map/all_to_all | solution.py:70
  57.9 4.2 %reshape.286 = bf16[128,2,5376]{2,1,0:T(2,128)(2,1)} reshape(bf16[128,10752]{1,0:T(8,128)(2,1)} %reduce) | data formatting | bytes 5505024
  62.1 22.5 %all-to-all-start.1 = ((bf16[128,2,5376]{2,1,0:T(2,128)(2,1)}), bf16[128,2,5376]{2,1,0:T(2,128)(2,1)S(1)}, u32[]{:S(2)}, u32[]{:S(2)}) async-start(bf16[128,2,5376]{2,1,0:T(2,128)(2,1)} %reshape.286), calls=%async_computation.1 | async-start | bytes 5505024 | tf_op jit(solution)/shard_map/all_to_all | solution.py:70
  84.6 0.3 reduce-scatter.2.cloned.1.call-start
  84.9 0.1 constant_dynamic-slice_fusion.1
  84.9 0.1 copy.53
  85.0 0.1 broadcast_bitcast_fusion
  85.1 3.6 %convert_bitcast_fusion = f32[896,4,256]{2,0,1:T(8,128)} fusion(bf16[4,896,256]{2,1,0:T(8,128)(2,1)} %all-to-all-done.2), kind=kLoop, calls=%fused_computation.5 | loop fusion | flops 917504 | bytes 5505024 | tf_op jit(solution)/shard_map/convert_element_type | solution.py:53
  88.7 4.6 %copy.51 = f32[896,4,256]{0,2,1:T(8,128)} copy(f32[896,4,256]{2,0,1:T(8,128)} %convert_bitcast_fusion) | data formatting | bytes 7340032 | tf_op jit(solution)/shard_map/convert_element_type | solution.py:53
  93.3 4.5 %subtract_convert_fusion = (bf16[896,8,128]{0,2,1:T(8,128)(2,1)}, bf16[896,8,128]{0,2,1:T(8,128)(2,1)}) fusion(f32[896,8,128]{0,2,1:T(8,128)} %bitcast.62, f32[896,8]{0,1:T(8,128)S(1)} %broadcast_bitcast_fusion), kind=kLoop, calls=%fused_computation.6 | loop fusion | flops 4587520 | bytes 7368704 | tf_op jit(solution)/shard_map/convert_element_type | solution.py:55
  97.9 52.3 %all-to-all-done.1 = bf16[128,2,5376]{2,1,0:T(2,128)(2,1)S(1)} async-done(((bf16[128,2,5376]{2,1,0:T(2,128)(2,1)}), bf16[128,2,5376]{2,1,0:T(2,128)(2,1)S(1)}, u32[]{:S(2)}, u32[]{:S(2)}) %all-to-all-start.1) | async-done | bytes 2752544 | tf_op jit(solution)/shard_map/all_to_all | solution.py:70
  150.1 7.1 %reshape.287 = bf16[128,1,10752]{2,1,0:T(2,128)(2,1)} reshape(bf16[128,2,5376]{2,1,0:T(2,128)(2,1)S(1)} %all-to-all-done.1) | data formatting | bytes 5505024
  157.2 2.9 copy.59
  160.2 1.5 copy-done.2
  161.7 0.1 slice.25
  161.8 1.5 reshape.226
  163.3 2.6 fusion.10
  165.9 2.6 convolution_add_fusion
  168.6 1.6 slice.24
  170.2 2.9 gather_fusion.2
  173.1 3.0 broadcast_select_fusion
  176.1 21.2 %reduce-scatter.2.cloned.1.call-done = f32[512,256]{1,0:T(8,128)} async-done(((f32[512,1024]{1,0:T(8,128)}), f32[512,256]{1,0:T(8,128)}) %reduce-scatter.2.cloned.1.call-update) | async-done | bytes 524304 | tf_op jit(solution)/shard_map/reduce_scatter | solution.py:83
  197.3 1.2 multiply_convert_fusion.1
  198.5 0.2 reshape.230
  198.6 1.6 maximum_bitcast_fusion.1
  200.3 2.9 reduce.1
  203.2 4.5 %reshape.288 = bf16[128,2,4096]{2,1,0:T(2,128)(2,1)} reshape(bf16[128,8192]{1,0:T(8,128)(2,1)} %reduce.1) | data formatting | bytes 4194304
  207.7 14.5 %all-to-all-start.4 = ((bf16[128,2,4096]{2,1,0:T(2,128)(2,1)}), bf16[128,2,4096]{2,1,0:T(2,128)(2,1)S(1)}, u32[]{:S(2)}, u32[]{:S(2)}) async-start(bf16[128,2,4096]{2,1,0:T(2,128)(2,1)} %reshape.288), calls=%async_computation.5 | async-start | bytes 4194304 | tf_op jit(solution)/shard_map/all_to_all | solution.py:86
  222.2 0.1 copy.45
  222.3 52.0 %all-to-all-done.4 = bf16[128,2,4096]{2,1,0:T(2,128)(2,1)S(1)} async-done(((bf16[128,2,4096]{2,1,0:T(2,128)(2,1)}), bf16[128,2,4096]{2,1,0:T(2,128)(2,1)S(1)}, u32[]{:S(2)}, u32[]{:S(2)}) %all-to-all-start.4) | async-done | bytes 2097184 | tf_op jit(solution)/shard_map/all_to_all | solution.py:86
  274.3 6.8 %reshape.289 = bf16[128,1,8192]{2,1,0:T(2,128)(2,1)} reshape(bf16[128,2,4096]{2,1,0:T(2,128)(2,1)S(1)} %all-to-all-done.4) | data formatting | bytes 4194304
  281.1 4.5 %copy.60 = bf16[128,1,8192]{2,0,1:T(8,128)(2,1)S(1)} copy(bf16[128,1,8192]{2,1,0:T(2,128)(2,1)} %reshape.289) | data formatting | bytes 4194304
  285.6 0.1 slice.27
  285.8 0.2 reshape.231
  285.9 3.3 %broadcast_in_dim_reshape.4 = bf16[1,3584,256]{2,1,0:T(8,128)(2,1)} reshape(bf16[128,7168]{1,0:T(8,128)(2,1)S(1)} %slice.27) | data formatting | bytes 3670016 | tf_op jit(solution)/shard_map/broadcast_in_dim;reshape | solution.py:97
  289.2 1.1 gather_fusion.3
  290.4 0.8 fusion
  (32 shorter events, 0.2 us)
Async XLA Ops:
  7.2 3.2 %copy-start = (f32[128,28,2]{0,2,1:T(2,128)S(1)}, f32[128,28,2]{0,2,1:T(2,128)}, u32[]{:S(2)}) copy-start(f32[128,28,2]{0,2,1:T(2,128)} %param.11) | copy-start | bytes 86020
  11.2 18.6 %all-to-all-start.3 = ((f32[4,28,2]{1,2,0:T(2,128)}), f32[4,28,2]{1,2,0:T(2,128)S(1)}, u32[]{:S(2)}, u32[]{:S(2)}) async-start(f32[4,28,2]{1,2,0:T(2,128)} %stack.3), calls=%async_computation.3 | async-start | bytes 8192 | tf_op jit(solution)/shard_map/all_to_all | solution.py:48
  29.8 8.7 %all-to-all-start = ((bf16[4,2,3584]{2,1,0:T(2,128)(2,1)}), bf16[4,2,3584]{2,1,0:T(2,128)(2,1)S(1)}, u32[]{:S(2)}, u32[]{:S(2)}) async-start(bf16[4,2,3584]{2,1,0:T(2,128)(2,1)} %reshape.284), calls=%async_computation | async-start | bytes 114688 | tf_op jit(solution)/shard_map/all_to_all | solution.py:56
  38.6 23.6 %all-to-all-start.2 = ((bf16[4,896,256]{2,1,0:T(8,128)(2,1)}), bf16[4,896,256]{2,1,0:T(8,128)(2,1)}, u32[]{:S(2)}, u32[]{:S(2)}) async-start(bf16[4,896,256]{2,1,0:T(8,128)(2,1)} %bitcast.10), calls=%async_computation.2 | async-start | bytes 3670016 | tf_op jit(solution)/shard_map/all_to_all | solution.py:45
  62.1 88.0 %all-to-all-start.1 = ((bf16[128,2,5376]{2,1,0:T(2,128)(2,1)}), bf16[128,2,5376]{2,1,0:T(2,128)(2,1)S(1)}, u32[]{:S(2)}, u32[]{:S(2)}) async-start(bf16[128,2,5376]{2,1,0:T(2,128)(2,1)} %reshape.286), calls=%async_computation.1 | async-start | bytes 5505024 | tf_op jit(solution)/shard_map/all_to_all | solution.py:70
  84.6 112.7 %reduce-scatter.2.cloned.1.call-start = ((), (), s32[]{:S(2)}) async-start(), calls=%async_computation.6 | async-start | bytes 2621440 | tf_op jit(solution)/shard_map/reduce_scatter | solution.py:83
  160.2 1.6 copy-start.2
  160.2 3.1 %copy-start.4 = (bf16[896,8,128]{0,2,1:T(8,128)(2,1)S(1)}, bf16[896,8,128]{0,2,1:T(8,128)(2,1)}, u32[]{:S(2)}) copy-start(bf16[896,8,128]{0,2,1:T(8,128)(2,1)} %get-tuple-element.5) | copy-start | bytes 5505028
  163.3 2.6 copy-start.3
  163.3 2.6 copy-start.5
  207.7 14.5 %copy-start.6 = (f32[2,16,8]{1,2,0:T(8,128)S(1)}, f32[2,16,8]{1,2,0:T(8,128)}, u32[]{:S(2)}) copy-start(f32[2,16,8]{1,2,0:T(8,128)} %param.9) | copy-start | bytes 3076
  207.7 66.6 %all-to-all-start.4 = ((bf16[128,2,4096]{2,1,0:T(2,128)(2,1)}), bf16[128,2,4096]{2,1,0:T(2,128)(2,1)S(1)}, u32[]{:S(2)}, u32[]{:S(2)}) async-start(bf16[128,2,4096]{2,1,0:T(2,128)(2,1)} %reshape.288), calls=%async_computation.5 | async-start | bytes 4194304 | tf_op jit(solution)/shard_map/all_to_all | solution.py:86
  285.8 5.4 %copy-start.1 = (f32[128,28,2]{0,2,1:T(2,128)S(1)}, f32[128,28,2]{0,2,1:T(2,128)}, u32[]{:S(2)}) copy-start(f32[128,28,2]{0,2,1:T(2,128)} %param.11) | copy-start | bytes 86020
Sparse Core Ops, SparseCore 0:
  168.7 28.5 reduce-scatter.1
